TPU v7x, 32 devices: a whole 2x2x4 slice. The times are simulated.
32 devices in a mesh: groups: 2 (over x), dp: 16 (over z, y, core).
Axes of the slice: x: 2, y: 2, z: 4, core: 2. Of those that a mesh axis runs over, the one named last changes fastest.
Arguments:
- frames: bfloat16 [128, 256, 1536], P(('groups', 'dp')), parts along dimension 0, may hold values from -6 to 6
- cotangent: bfloat16 [128, 256, 1536], P(('groups', 'dp')), parts along dimension 0, may hold values from -6 to 6
- gain: float32 [1536], replicated, may hold values from 0.25 to 1.75
- down_weight: bfloat16 [320, 1536, 256], P('groups', 'dp'), parts along dimension 0, may hold values from -0.15625 to 0.15625
- up_weight: bfloat16 [320, 1536, 256], P('groups', 'dp'), parts along dimension 0, may hold values from -0.375 to 0.375
- slot_lang: int32 [32, 2], P('groups'), parts along dimension 0, may hold values from 0 to 159
- utt_slot: int32 [128], P('groups'), parts along dimension 0, may hold values from 0 to 1
- lengths: int32 [128], P('groups'), parts along dimension 0, may hold values from 64 to 256
Outputs:
- frame_grads: bfloat16 [128, 256, 1536], P(('groups', 'dp')), parts along dimension 0
- down_grads: bfloat16 [320, 1536, 256], P('groups', 'dp'), parts along dimension 0
- up_grads: bfloat16 [320, 1536, 256], P('groups', 'dp'), parts along dimension 0
There are 2 independent parts, one for each index of `groups`. A program takes and returns all parts, laid end to end along the dimension named above; an argument that names none is the same for every part. Nothing has to cross between parts.
All inputs are finite; a program needn't handle non-finite values.
Results may differ from a plain program's by a relative error of at most 0.0061.
Values may be sent and summed in bfloat16 or wider, within the bound.
No kernel may reach another device: no remote copies, remote signals or barrier semaphores. Data moves between devices by JAX's collectives and lax.ppermute only.
A program may use at most 128 MiB of HBM per device.

v0:
```python
import jax
import jax.numpy as jnp
from jax import lax
from jax.sharding import PartitionSpec as P


def local_pass(frames, cotangent, gain, w_down, w_up, live_mask, slot_select):
    values = frames.astype(jnp.float32)
    centre_mean = jnp.mean(values, axis=2, keepdims=True)
    mean_removed = values - centre_mean
    variance = jnp.mean(mean_removed * mean_removed, axis=2, keepdims=True)
    reciprocal_deviation = lax.rsqrt(variance + 1e-06)
    standardized_input = mean_removed * reciprocal_deviation
    layer_normed = (standardized_input * gain).astype(jnp.bfloat16)
    pre_act = jnp.einsum("ufd,udr->ufr", layer_normed, w_down, preferred_element_type=jnp.float32)
    sigmoid_pre = jax.nn.sigmoid(pre_act)
    hidden = (pre_act * sigmoid_pre).astype(jnp.bfloat16)
    masked_up = jnp.where(live_mask, cotangent, jnp.zeros_like(cotangent))
    hidden_slots = hidden[None] * slot_select[:, :, None, None]
    grad_up = jnp.einsum(
        "ufd,sufr->sdr", masked_up, hidden_slots, preferred_element_type=jnp.float32
    )
    d_hidden = jnp.einsum("ufd,udr->ufr", masked_up, w_up, preferred_element_type=jnp.float32)
    d_pre = (d_hidden * sigmoid_pre * (1.0 + pre_act * (1.0 - sigmoid_pre))).astype(jnp.bfloat16)
    d_pre_slots = d_pre[None] * slot_select[:, :, None, None]
    grad_down = jnp.einsum(
        "ufd,sufr->sdr", layer_normed, d_pre_slots, preferred_element_type=jnp.float32
    )
    d_normed = jnp.einsum("ufr,udr->ufd", d_pre, w_down, preferred_element_type=jnp.float32)
    scaled_rows = d_normed * gain
    inner_gradient = (
        scaled_rows
        - jnp.mean(scaled_rows, axis=2, keepdims=True)
        - standardized_input * jnp.mean(scaled_rows * standardized_input, axis=2, keepdims=True)
    ) * reciprocal_deviation
    d_frames = (cotangent.astype(jnp.float32) + inner_gradient).astype(jnp.bfloat16)
    return (d_frames, grad_down, grad_up)


def on_device(frames, cotangent, gain, down_weight, up_weight, slot_lang, utt_slot, lengths):
    devices = lax.axis_size("dp")
    self_index = lax.axis_index("dp")
    per_device = frames.shape[0]
    slots = slot_lang.shape[1]
    lang_count, row_count, bottleneck = down_weight.shape
    owners = jnp.arange(utt_slot.shape[0], dtype=jnp.int32) // per_device
    utt_lang = slot_lang[owners, utt_slot]
    own_lengths = lax.dynamic_slice_in_dim(lengths, self_index * per_device, per_device)
    own_slot = lax.dynamic_slice_in_dim(utt_slot, self_index * per_device, per_device)
    live_mask = (jnp.arange(frames.shape[1], dtype=jnp.int32)[None, :] < own_lengths[:, None])[
        :, :, None
    ]
    lang_ids = jnp.arange(lang_count, dtype=jnp.int32)
    counts = jnp.sum(jnp.where(utt_lang[None, :] == lang_ids[:, None], lengths[None, :], 0), axis=1)
    scaling = lax.rsqrt(jnp.maximum(counts, 1).astype(jnp.float32))
    member_langs = slot_lang.T.reshape(-1)
    send_down = jnp.take(down_weight, member_langs, axis=0).reshape(
        slots, devices, row_count, bottleneck
    )
    send_up = jnp.take(up_weight, member_langs, axis=0).reshape(
        slots, devices, row_count, bottleneck
    )
    got_down = lax.all_to_all(send_down, "dp", split_axis=1, concat_axis=1, tiled=True)
    got_up = lax.all_to_all(send_up, "dp", split_axis=1, concat_axis=1, tiled=True)
    got_down = got_down.reshape(slots, devices * row_count, bottleneck)
    got_up = got_up.reshape(slots, devices * row_count, bottleneck)
    w_down = jnp.take(got_down, own_slot, axis=0)
    w_up = jnp.take(got_up, own_slot, axis=0)
    slot_select = (jnp.arange(slots, dtype=jnp.int32)[:, None] == own_slot[None, :]).astype(
        jnp.bfloat16
    )
    d_frames, grad_down, grad_up = local_pass(
        frames, cotangent, gain, w_down, w_up, live_mask, slot_select
    )
    own_scale = jnp.take(scaling, lax.dynamic_index_in_dim(slot_lang, self_index, 0, False))
    own_scale = own_scale[:, None, None]

    def exchange_back(grad):
        scaled = (grad * own_scale).astype(jnp.bfloat16)
        scaled = scaled.reshape(slots, devices, row_count, bottleneck)
        back = lax.all_to_all(scaled, "dp", split_axis=1, concat_axis=1, tiled=True)
        return back.reshape(slots * devices, row_count, bottleneck)

    back_down = exchange_back(grad_down)
    back_up = exchange_back(grad_up)
    lang_table = (lang_ids[:, None] == member_langs[None, :]).astype(jnp.bfloat16)
    down_grads = jnp.einsum(
        "lm,mkr->lkr", lang_table, back_down, preferred_element_type=jnp.float32
    ).astype(jnp.bfloat16)
    up_grads = jnp.einsum(
        "lm,mkr->lkr", lang_table, back_up, preferred_element_type=jnp.float32
    ).astype(jnp.bfloat16)
    return (d_frames, down_grads, up_grads)


def solution(mesh):
    placed = (
        P(("groups", "dp"), None, None),
        P(("groups", "dp"), None, None),
        P(),
        P("groups", "dp", None),
        P("groups", "dp", None),
        P("groups", None),
        P("groups"),
        P("groups"),
    )
    return jax.shard_map(
        on_device,
        mesh=mesh,
        in_specs=placed,
        out_specs=(
            P(("groups", "dp"), None, None),
            P("groups", "dp", None),
            P("groups", "dp", None),
        ),
        check_vma=False,
    )
```

profile of v0, /device:TPU:13, one launch (start us, length us, event | category | flops | bytes accessed | tf_op | source)
XLA Modules:
  0.0 215.7 jit_solution(16785040773158458793)
XLA Ops:
  1.4 3.9 %gather_fusion.4 = bf16[32,96,256]{2,1,0:T(8,128)(2,1)S(1)} fusion(bf16[160,96,256]{2,1,0:T(8,128)(2,1)} %param.15, s32[1024]{0:T(1024)S(1)} %pad_clamp_fusion.2), kind=kCustom, calls=%fused_computation.2.clone | custom fusion | bytes 3145856 | tf_op jit(solution)/shard_map/jit(_take)/gather | solution.py:57
  5.3 3.9 %gather_fusion.2 = bf16[32,96,256]{2,1,0:T(8,128)(2,1)S(1)} fusion(bf16[160,96,256]{2,1,0:T(8,128)(2,1)} %param.16, s32[1024]{0:T(1024)S(1)} %pad_clamp_fusion.2), kind=kCustom, calls=%fused_computation.clone | custom fusion | bytes 3145856 | tf_op jit(solution)/shard_map/jit(_take)/gather | solution.py:60
  12.0 6.6 %all-to-all-start.1 = ((bf16[2,16,96,256]{3,2,0,1:T(8,128)(2,1)}), bf16[2,16,96,256]{3,2,0,1:T(8,128)(2,1)}, u32[]{:S(2)}, u32[]{:S(2)}) async-start(bf16[2,16,96,256]{3,2,0,1:T(8,128)(2,1)} %copy.51), calls=%async_computation.1 | async-start | bytes 3145728 | tf_op jit(solution)/shard_map/all_to_all | solution.py:63
  18.6 2.8 %copy.49 = bf16[2,16,96,256]{3,2,0,1:T(8,128)(2,1)} copy(bf16[2,16,96,256]{3,2,1,0:T(8,128)(2,1)} %bitcast.69) | data formatting | bytes 3145728 | tf_op jit(solution)/shard_map/reshape | solution.py:60
  21.4 33.4 %all-to-all-done.1 = bf16[2,16,96,256]{3,2,0,1:T(8,128)(2,1)} async-done(((bf16[2,16,96,256]{3,2,0,1:T(8,128)(2,1)}), bf16[2,16,96,256]{3,2,0,1:T(8,128)(2,1)}, u32[]{:S(2)}, u32[]{:S(2)}) %all-to-all-start.1) | async-done | bytes 1572896 | tf_op jit(solution)/shard_map/all_to_all | solution.py:63
  54.8 4.9 %all-to-all-start = ((bf16[2,16,96,256]{3,2,0,1:T(8,128)(2,1)}), bf16[2,16,96,256]{3,2,0,1:T(8,128)(2,1)}, u32[]{:S(2)}, u32[]{:S(2)}) async-start(bf16[2,16,96,256]{3,2,0,1:T(8,128)(2,1)} %copy.49), calls=%async_computation | async-start | bytes 3145728 | tf_op jit(solution)/shard_map/all_to_all | solution.py:64
  63.3 2.7 %copy.52 = bf16[2,16,96,256]{3,2,1,0:T(8,128)(2,1)} copy(bf16[2,16,96,256]{3,2,0,1:T(8,128)(2,1)} %all-to-all-done.1) | data formatting | bytes 3145728 | tf_op jit(solution)/shard_map/all_to_all | solution.py:63
  66.0 3.8 %gather_fusion.5 = bf16[4,1536,256]{2,1,0:T(8,128)(2,1)} fusion(bf16[2,1536,256]{2,1,0:T(8,128)(2,1)} %bitcast.64, s32[1024]{0:T(1024)S(1)} %pad_clamp_fusion.1), kind=kCustom, calls=%fused_computation.3.clone | custom fusion | bytes 6291472 | tf_op jit(solution)/shard_map/jit(_take)/gather | solution.py:67
  69.8 26.2 %all-to-all-done = bf16[2,16,96,256]{3,2,0,1:T(8,128)(2,1)} async-done(((bf16[2,16,96,256]{3,2,0,1:T(8,128)(2,1)}), bf16[2,16,96,256]{3,2,0,1:T(8,128)(2,1)}, u32[]{:S(2)}, u32[]{:S(2)}) %all-to-all-start) | async-done | bytes 1572896 | tf_op jit(solution)/shard_map/all_to_all | solution.py:64
  96.0 2.7 %copy.50 = bf16[2,16,96,256]{3,2,1,0:T(8,128)(2,1)} copy(bf16[2,16,96,256]{3,2,0,1:T(8,128)(2,1)} %all-to-all-done) | data formatting | bytes 3145728 | tf_op jit(solution)/shard_map/all_to_all | solution.py:64
  98.7 3.8 %gather_fusion.3 = bf16[4,1536,256]{2,1,0:T(8,128)(2,1)} fusion(bf16[2,1536,256]{2,1,0:T(8,128)(2,1)} %bitcast.63, s32[1024]{0:T(1024)S(1)} %pad_clamp_fusion.1), kind=kCustom, calls=%fused_computation.1.clone | custom fusion | bytes 6291472 | tf_op jit(solution)/shard_map/jit(_take)/gather | solution.py:68
  102.5 4.4 %multiply_convert_fusion = (bf16[4,256,256]{2,1,0:T(8,128)(2,1)}, f32[4,256,256]{2,1,0:T(8,128)S(1)}) fusion(bf16[4,1536,256]{2,1,0:T(8,128)(2,1)} %gather_fusion.5, pred[4]{0:T(512)(128)(4,1)S(1)} %get-tuple-element.22, bf16[4,256,1536]{2,1,0:T(8,128)(2,1)S(1)} %copy-done.1, f32[1536]{0:T(1024)S(1)} %copy-done.5, f32[4,256]{1,0:T(4,128)S(1)} %add_rsqrt_fusion, ...), kind=kOutput, calls=%fused_computation.49 | convolution fusion | flops 816054272 | bytes 7878660 | tf_op jit(solution)/shard_map/ufd,udr->ufr/dot_general | solution.py:15
  111.1 4.2 %fusion.28 = bf16[2,1536,256]{1,2,0:T(8,128)(2,1)} fusion(bf16[4,256,1536]{2,1,0:T(8,128)(2,1)S(1)} %copy-done.1, f32[1536]{0:T(1024)S(1)} %copy-done.5, f32[4,256]{1,0:T(4,128)S(1)} %add_rsqrt_fusion, f32[4,256]{1,0:T(4,128)S(1)} %broadcast_multiply_fusion.2, f32[2]{0:T(128)S(1)} %and_select_fusion.1, bf16[2,4]{1,0:T(2,128)(2,1)S(1)} %compare_convert_fusion, ...), kind=kOutput, calls=%fused_computation.37 | convolution fusion | flops 1620574208 | bytes 5257240 | tf_op jit(solution)/shard_map/ufd,sufr->sdr/dot_general | solution.py:26
  117.9 2.7 %copy.55 = bf16[2,16,96,256]{3,2,0,1:T(8,128)(2,1)} copy(bf16[2,16,96,256]{3,2,1,0:T(8,128)(2,1)} %bitcast.66) | data formatting | bytes 3145728 | tf_op jit(solution)/shard_map/reshape | solution.py:80
  120.6 4.9 %all-to-all-start.2 = ((bf16[2,16,96,256]{3,2,0,1:T(8,128)(2,1)}), bf16[2,16,96,256]{3,2,0,1:T(8,128)(2,1)}, u32[]{:S(2)}, u32[]{:S(2)}) async-start(bf16[2,16,96,256]{3,2,0,1:T(8,128)(2,1)} %copy.55), calls=%async_computation.2 | async-start | bytes 3145728 | tf_op jit(solution)/shard_map/all_to_all | solution.py:81
  127.6 5.1 %fusion.25 = bf16[2,1536,256]{1,2,0:T(8,128)(2,1)} fusion(bf16[4,256,1536]{2,1,0:T(8,128)(2,1)} %param.13, pred[4,256]{1,0:T(4,128)(4,1)S(1)} %iota_compare_fusion.2, f32[2]{0:T(128)S(1)} %and_select_fusion.1, bf16[4,256,256]{1,2,0:T(8,128)(2,1)} %copy.57, bf16[2,4]{1,0:T(2,128)(2,1)S(1)} %compare_convert_fusion), kind=kOutput, calls=%fused_computation.36 | convolution fusion | flops 1614282752 | bytes 5243928 | tf_op jit(solution)/shard_map/ufd,sufr->sdr/dot_general | solution.py:20
  135.2 2.7 %copy.59 = bf16[2,16,96,256]{3,2,0,1:T(8,128)(2,1)} copy(bf16[2,16,96,256]{3,2,1,0:T(8,128)(2,1)} %bitcast.67) | data formatting | bytes 3145728 | tf_op jit(solution)/shard_map/reshape | solution.py:80
  137.9 23.9 %all-to-all-done.2 = bf16[2,16,96,256]{3,2,0,1:T(8,128)(2,1)} async-done(((bf16[2,16,96,256]{3,2,0,1:T(8,128)(2,1)}), bf16[2,16,96,256]{3,2,0,1:T(8,128)(2,1)}, u32[]{:S(2)}, u32[]{:S(2)}) %all-to-all-start.2) | async-done | bytes 1572896 | tf_op jit(solution)/shard_map/all_to_all | solution.py:81
  161.8 4.9 %all-to-all-start.3 = ((bf16[2,16,96,256]{3,2,0,1:T(8,128)(2,1)}), bf16[2,16,96,256]{3,2,0,1:T(8,128)(2,1)}, u32[]{:S(2)}, u32[]{:S(2)}) async-start(bf16[2,16,96,256]{3,2,0,1:T(8,128)(2,1)} %copy.59), calls=%async_computation.3 | async-start | bytes 3145728 | tf_op jit(solution)/shard_map/all_to_all | solution.py:81
  166.7 4.6 %multiply_reduce_fusion = (f32[4,256]{1,0:T(4,128)S(1)}, f32[4,256]{1,0:T(4,128)S(1)}, f32[4,256,1536]{2,1,0:T(8,128)S(1)}) fusion(f32[1536]{0:T(1024)S(1)} %copy-done.5, f32[4,256]{1,0:T(4,128)S(1)} %add_rsqrt_fusion, f32[4,256]{1,0:T(4,128)S(1)} %broadcast_multiply_fusion.2, bf16[4,256,1536]{2,1,0:T(8,128)(2,1)S(1)} %copy-done.1, ...), kind=kOutput, calls=%fused_computation.22 | convolution fusion | flops 817887232 | bytes 13129732 | tf_op jit(solution)/shard_map/ufr,udr->ufd/dot_general | solution.py:29
  171.4 4.0 %fusion.10 = bf16[4,256,1536]{2,1,0:T(8,128)(2,1)} fusion(bf16[4,256,1536]{2,1,0:T(8,128)(2,1)S(1)} %copy-done.1, bf16[4,256,1536]{2,1,0:T(8,128)(2,1)S(1)} %copy-done.4, f32[4,256,1536]{2,1,0:T(8,128)S(1)} %get-tuple-element.26, f32[4,256]{1,0:T(4,128)S(1)} %get-tuple-element.29, f32[4,256]{1,0:T(4,128)S(1)} %get-tuple-element.30, f32[1536]{0:T(1024)S(1)} %copy-done.5, ...), kind=kLoop, calls=%fused_computation.20 | loop fusion | flops 17301504 | bytes 15751168 | tf_op jit(solution)/shard_map/convert_element_type | solution.py:36
  179.9 7.8 %copy.61 = bf16[160,96,256]{2,1,0:T(8,128)(2,1)} copy(bf16[160,96,256]{2,0,1:T(8,128)(2,1)S(1)} %convolution_convert_fusion.1) | data formatting | bytes 15728640
  187.7 15.3 %all-to-all-done.3 = bf16[2,16,96,256]{3,2,0,1:T(8,128)(2,1)} async-done(((bf16[2,16,96,256]{3,2,0,1:T(8,128)(2,1)}), bf16[2,16,96,256]{3,2,0,1:T(8,128)(2,1)}, u32[]{:S(2)}, u32[]{:S(2)}) %all-to-all-start.3) | async-done | bytes 1572896 | tf_op jit(solution)/shard_map/all_to_all | solution.py:81
  207.6 8.1 %copy.62 = bf16[160,96,256]{2,1,0:T(8,128)(2,1)} copy(bf16[160,96,256]{2,0,1:T(8,128)(2,1)S(1)} %convolution_convert_fusion) | data formatting | bytes 15728640
  (51 shorter events, 27.7 us)
Async XLA Ops:
  12.0 42.8 %all-to-all-start.1 = ((bf16[2,16,96,256]{3,2,0,1:T(8,128)(2,1)}), bf16[2,16,96,256]{3,2,0,1:T(8,128)(2,1)}, u32[]{:S(2)}, u32[]{:S(2)}) async-start(bf16[2,16,96,256]{3,2,0,1:T(8,128)(2,1)} %copy.51), calls=%async_computation.1 | async-start | bytes 3145728 | tf_op jit(solution)/shard_map/all_to_all | solution.py:63
  18.5 41.2 %copy-start.7 = (s32[64]{0:T(128)S(1)}, s32[64]{0:T(128)}, u32[]{:S(2)}) copy-start(s32[64]{0:T(128)} %param.18) | copy-start | bytes 772
  18.5 41.2 %copy-start = (s32[16,2]{0,1:T(2,128)S(1)}, s32[16,2]{0,1:T(2,128)}, u32[]{:S(2)}) copy-start(s32[16,2]{0,1:T(2,128)} %param.17) | copy-start | bytes 388
  18.5 42.3 %copy-start.6 = (s32[64]{0:T(128)S(1)}, s32[64]{0:T(128)}, u32[]{:S(2)}) copy-start(s32[64]{0:T(128)} %param.19) | copy-start | bytes 772
  18.5 43.3 %copy-start.1 = (bf16[4,256,1536]{2,1,0:T(8,128)(2,1)S(1)}, bf16[4,256,1536]{2,1,0:T(8,128)(2,1)}, u32[]{:S(2)}) copy-start(bf16[4,256,1536]{2,1,0:T(8,128)(2,1)} %param.12) | copy-start | bytes 9437188
  54.8 41.2 %all-to-all-start = ((bf16[2,16,96,256]{3,2,0,1:T(8,128)(2,1)}), bf16[2,16,96,256]{3,2,0,1:T(8,128)(2,1)}, u32[]{:S(2)}, u32[]{:S(2)}) async-start(bf16[2,16,96,256]{3,2,0,1:T(8,128)(2,1)} %copy.49), calls=%async_computation | async-start | bytes 3145728 | tf_op jit(solution)/shard_map/all_to_all | solution.py:64
  98.7 3.8 %copy-start.5 = (f32[1536]{0:T(1024)S(1)}, f32[1536]{0:T(1024)}, u32[]{:S(2)}) copy-start(f32[1536]{0:T(1024)} %param.14) | copy-start | bytes 18436
  102.5 4.4 %copy-start.2 = (bf16[4,1536,256]{2,1,0:T(8,128)(2,1)S(1)}, bf16[4,1536,256]{2,1,0:T(8,128)(2,1)}, u32[]{:S(2)}) copy-start(bf16[4,1536,256]{2,1,0:T(8,128)(2,1)} %gather_fusion.3) | copy-start | bytes 9437188
  102.5 4.4 %copy-start.3 = (bf16[4,256,1536]{2,1,0:T(8,128)(2,1)S(1)}, bf16[4,256,1536]{2,1,0:T(8,128)(2,1)}, u32[]{:S(2)}) copy-start(bf16[4,256,1536]{2,1,0:T(8,128)(2,1)} %param.13) | copy-start | bytes 9437188
  120.6 41.2 %all-to-all-start.2 = ((bf16[2,16,96,256]{3,2,0,1:T(8,128)(2,1)}), bf16[2,16,96,256]{3,2,0,1:T(8,128)(2,1)}, u32[]{:S(2)}, u32[]{:S(2)}) async-start(bf16[2,16,96,256]{3,2,0,1:T(8,128)(2,1)} %copy.55), calls=%async_computation.2 | async-start | bytes 3145728 | tf_op jit(solution)/shard_map/all_to_all | solution.py:81
  161.8 41.2 %all-to-all-start.3 = ((bf16[2,16,96,256]{3,2,0,1:T(8,128)(2,1)}), bf16[2,16,96,256]{3,2,0,1:T(8,128)(2,1)}, u32[]{:S(2)}, u32[]{:S(2)}) async-start(bf16[2,16,96,256]{3,2,0,1:T(8,128)(2,1)} %copy.59), calls=%async_computation.3 | async-start | bytes 3145728 | tf_op jit(solution)/shard_map/all_to_all | solution.py:81
  166.7 4.6 %copy-start.4 = (bf16[4,256,1536]{2,1,0:T(8,128)(2,1)S(1)}, bf16[4,256,1536]{2,1,0:T(8,128)(2,1)}, u32[]{:S(2)}) copy-start(bf16[4,256,1536]{2,1,0:T(8,128)(2,1)} %param.13) | copy-start | bytes 9437188
where the time goes:
time: 217 us; the launch traced here: 216 us
  waiting for transfers between devices  98.8 us (46%)
  local copies, waits for them, and re-layouts  62.5 us (29%)
  matrix products  25.1 us (12%)
  starting transfers between devices  21.3 us (10%)
  other arithmetic  7.25 us (3%)
    all_to_all x2, waiting for transfers between devices, exchange_back(): back = lax.all_to_all(scaled, 'dp', split_axis=1, concat_axis=1, tiled=True)  39.2 us
    all_to_all x1, waiting for transfers between devices, on_device(): lax.all_to_all(send_down, 'dp', split_axis=1, concat_axis=1, tiled=True)  33.4 us
    all_to_all x1, waiting for transfers between devices, on_device(): lax.all_to_all(send_up, 'dp', split_axis=1, concat_axis=1, tiled=True)  26.2 us
    unnamed x18, local copies, waits for them, and re-layouts  15.9 us
    all_to_all x2, starting transfers between devices, exchange_back(): back = lax.all_to_all(scaled, 'dp', split_axis=1, concat_axis=1, tiled=True)  9.83 us
    all_to_all x1, starting transfers between devices, on_device(): lax.all_to_all(send_down, 'dp', split_axis=1, concat_axis=1, tiled=True)  6.55 us
    reshape x2, local copies, waits for them, and re-layouts, exchange_back(): scaled = scaled.reshape(slots, devices, row_count, bottleneck)  5.37 us
    convert_element_type x2, local copies, waits for them, and re-layouts, exchange_back(): scaled = (grad * own_scale).astype(jnp.bfloat16)  5.15 us
  transfers between devices with their start and end apart: 4, of which 4 were waited for; matrix products, arithmetic and copies ran while one was open for 21% of the time, Pallas kernels for 0%

commit v1 on v0

--- a/solution.py
+++ b/solution.py
@@ -61,7 +61,10 @@
         slots, devices, row_count, bottleneck
     )
     got_down = lax.all_to_all(send_down, "dp", split_axis=1, concat_axis=1, tiled=True)
-    got_up = lax.all_to_all(send_up, "dp", split_axis=1, concat_axis=1, tiled=True)
+    got_up = jnp.concatenate(
+        lax.all_to_all(jnp.stack(jnp.split(send_up, lax.axis_size("dp"), axis=1)), "dp", 0, 0),
+        axis=1,
+    )
     got_down = got_down.reshape(slots, devices * row_count, bottleneck)
     got_up = got_up.reshape(slots, devices * row_count, bottleneck)
     w_down = jnp.take(got_down, own_slot, axis=0)

time: 217 us -> 229 us (1.055)
  local copies, waits for them, and re-layouts: 62.5 us -> 71.6 us
  waiting for transfers between devices: 98.8 us -> 103 us
    unnamed x18 -> x33, local copies, waits for them, and re-layouts: 15.9 us -> 25.6 us
    all_to_all x1, waiting for transfers between devices: 26.2 us -> 33.2 us  [on_device(): lax.all_to_all(jnp.stack(jnp.split(send_up, lax.axis_size('dp'), axis=1))...]
    all_to_all x1, waiting for transfers between devices: 33.4 us -> 30.2 us  [on_device(): lax.all_to_all(send_down, 'dp', split_axis=1, concat_axis=1, tiled=True)]
    all_to_all x1 -> x0, local copies, waits for them, and re-layouts: 2.66 us -> none  [on_device(): lax.all_to_all(send_up, 'dp', split_axis=1, concat_axis=1, tiled=True)]
  transfers between devices with their start and end apart: 4 -> 4, of which waited for: 4 -> 4; matrix products, arithmetic and copies ran while one was open for 21% -> 19% of each run, Pallas kernels for 0% -> 0%
where the time goes in v1:
time: 229 us; the launch traced here: 228 us
  waiting for transfers between devices  103 us (45%)
  local copies, waits for them, and re-layouts  71.6 us (31%)
  matrix products  24.9 us (11%)
  starting transfers between devices  21.3 us (9%)
  other arithmetic  7.19 us (3%)
    all_to_all x2, waiting for transfers between devices, exchange_back(): back = lax.all_to_all(scaled, 'dp', split_axis=1, concat_axis=1, tiled=True)  39.2 us
    all_to_all x1, waiting for transfers between devices, on_device(): lax.all_to_all(jnp.stack(jnp.split(send_up, lax.axis_size('dp'), axis=1))...  33.2 us
    all_to_all x1, waiting for transfers between devices, on_device(): lax.all_to_all(send_down, 'dp', split_axis=1, concat_axis=1, tiled=True)  30.2 us
    unnamed x33, local copies, waits for them, and re-layouts  25.6 us
    all_to_all x2, starting transfers between devices, exchange_back(): back = lax.all_to_all(scaled, 'dp', split_axis=1, concat_axis=1, tiled=True)  9.81 us
    all_to_all x1, starting transfers between devices, on_device(): lax.all_to_all(jnp.stack(jnp.split(send_up, lax.axis_size('dp'), axis=1))...  6.55 us
    reshape x2, local copies, waits for them, and re-layouts, exchange_back(): scaled = scaled.reshape(slots, devices, row_count, bottleneck)  5.37 us
    convert_element_type x2, local copies, waits for them, and re-layouts, exchange_back(): scaled = (grad * own_scale).astype(jnp.bfloat16)  5.15 us
  transfers between devices with their start and end apart: 4, of which 4 were waited for; matrix products, arithmetic and copies ran while one was open for 19% of the time, Pallas kernels for 0%

profile of v1, /device:TPU:13, one launch (start us, length us, event | category | flops | bytes accessed | tf_op | source)
XLA Modules:
  0.0 228.4 jit_solution(17932134935132733881)
XLA Ops:
  1.4 3.9 %gather_fusion.4 = bf16[32,96,256]{2,1,0:T(8,128)(2,1)S(1)} fusion(bf16[160,96,256]{2,1,0:T(8,128)(2,1)} %param.15, s32[1024]{0:T(1024)S(1)} %pad_clamp_fusion.2), kind=kCustom, calls=%fused_computation.2.clone | custom fusion | bytes 3145856 | tf_op jit(solution)/shard_map/jit(_take)/gather | solution.py:57
  5.3 3.9 %gather_fusion.2 = bf16[32,96,256]{2,1,0:T(8,128)(2,1)S(1)} fusion(bf16[160,96,256]{2,1,0:T(8,128)(2,1)} %param.16, s32[1024]{0:T(1024)S(1)} %pad_clamp_fusion.2), kind=kCustom, calls=%fused_computation.clone | custom fusion | bytes 3145856 | tf_op jit(solution)/shard_map/jit(_take)/gather | solution.py:60
  21.0 6.6 %all-to-all-start = ((bf16[16,2,1,96,256]{4,3,1,2,0:T(8,128)(2,1)}), bf16[16,2,1,96,256]{4,3,1,2,0:T(8,128)(2,1)}, u32[]{:S(2)}, u32[]{:S(2)}) async-start(bf16[16,2,1,96,256]{4,3,1,2,0:T(8,128)(2,1)} %fusion.53), calls=%async_computation | async-start | bytes 3145728 | tf_op jit(solution)/shard_map/all_to_all | solution.py:65
  27.8 2.8 %copy.149 = bf16[2,16,96,256]{3,2,0,1:T(8,128)(2,1)} copy(bf16[2,16,96,256]{3,2,1,0:T(8,128)(2,1)} %bitcast.164) | data formatting | bytes 3145728 | tf_op jit(solution)/shard_map/reshape | solution.py:57
  30.7 33.2 %all-to-all-done = bf16[16,2,1,96,256]{4,3,1,2,0:T(8,128)(2,1)} async-done(((bf16[16,2,1,96,256]{4,3,1,2,0:T(8,128)(2,1)}), bf16[16,2,1,96,256]{4,3,1,2,0:T(8,128)(2,1)}, u32[]{:S(2)}, u32[]{:S(2)}) %all-to-all-start) | async-done | bytes 1572896 | tf_op jit(solution)/shard_map/all_to_all | solution.py:65
  63.9 4.9 %all-to-all-start.1 = ((bf16[2,16,96,256]{3,2,0,1:T(8,128)(2,1)}), bf16[2,16,96,256]{3,2,0,1:T(8,128)(2,1)}, u32[]{:S(2)}, u32[]{:S(2)}) async-start(bf16[2,16,96,256]{3,2,0,1:T(8,128)(2,1)} %copy.149), calls=%async_computation.1 | async-start | bytes 3145728 | tf_op jit(solution)/shard_map/all_to_all | solution.py:63
  72.2 2.7 %copy.148 = bf16[2,16,1,96,256]{4,3,1,0,2:T(8,128)(2,1)} copy(bf16[2,16,1,96,256]{4,3,0,2,1:T(8,128)(2,1)} %bitcast.18) | data formatting | bytes 3145728 | tf_op jit(solution)/shard_map/reshape | solution.py:64
  74.9 30.2 %all-to-all-done.1 = bf16[2,16,96,256]{3,2,0,1:T(8,128)(2,1)} async-done(((bf16[2,16,96,256]{3,2,0,1:T(8,128)(2,1)}), bf16[2,16,96,256]{3,2,0,1:T(8,128)(2,1)}, u32[]{:S(2)}, u32[]{:S(2)}) %all-to-all-start.1) | async-done | bytes 1572896 | tf_op jit(solution)/shard_map/all_to_all | solution.py:63
  105.1 2.7 %copy.150 = bf16[2,16,96,256]{3,2,1,0:T(8,128)(2,1)} copy(bf16[2,16,96,256]{3,2,0,1:T(8,128)(2,1)} %all-to-all-done.1) | data formatting | bytes 3145728 | tf_op jit(solution)/shard_map/all_to_all | solution.py:63
  107.8 3.8 %gather_fusion.5 = bf16[4,1536,256]{2,1,0:T(8,128)(2,1)} fusion(bf16[2,1536,256]{2,1,0:T(8,128)(2,1)} %bitcast.159, s32[1024]{0:T(1024)S(1)} %get-tuple-element.33), kind=kCustom, calls=%fused_computation.3.clone | custom fusion | bytes 6291472 | tf_op jit(solution)/shard_map/jit(_take)/gather | solution.py:70
  111.6 3.8 %gather_fusion.3 = bf16[4,1536,256]{2,1,0:T(8,128)(2,1)} fusion(bf16[2,1536,256]{2,1,0:T(8,128)(2,1)} %bitcast.158, s32[1024]{0:T(1024)S(1)} %get-tuple-element.33), kind=kCustom, calls=%fused_computation.1.clone | custom fusion | bytes 6291472 | tf_op jit(solution)/shard_map/jit(_take)/gather | solution.py:71
  115.4 4.4 %multiply_convert_fusion = (bf16[4,256,256]{2,1,0:T(8,128)(2,1)}, f32[4,256,256]{2,1,0:T(8,128)S(1)}) fusion(bf16[4,1536,256]{2,1,0:T(8,128)(2,1)} %gather_fusion.5, pred[4]{0:T(512)(128)(4,1)S(1)} %get-tuple-element.25, bf16[4,256,1536]{2,1,0:T(8,128)(2,1)S(1)} %copy-done.1, f32[1536]{0:T(1024)S(1)} %copy-done.5, f32[4,256]{1,0:T(4,128)S(1)} %add_rsqrt_fusion, ...), kind=kOutput, calls=%fused_computation.49 | convolution fusion | flops 816054272 | bytes 7878660 | tf_op jit(solution)/shard_map/ufd,udr->ufr/dot_general | solution.py:15
  124.0 4.1 %fusion.28 = bf16[2,1536,256]{1,2,0:T(8,128)(2,1)} fusion(bf16[4,256,1536]{2,1,0:T(8,128)(2,1)S(1)} %copy-done.1, f32[1536]{0:T(1024)S(1)} %copy-done.5, f32[4,256]{1,0:T(4,128)S(1)} %add_rsqrt_fusion, f32[4,256]{1,0:T(4,128)S(1)} %broadcast_multiply_fusion.2, f32[2]{0:T(128)S(1)} %and_select_fusion.1, bf16[2,4]{1,0:T(2,128)(2,1)S(1)} %compare_convert_fusion, ...), kind=kOutput, calls=%fused_computation.37 | convolution fusion | flops 1620574208 | bytes 5257240 | tf_op jit(solution)/shard_map/ufd,sufr->sdr/dot_general | solution.py:26
  130.7 2.7 %copy.153 = bf16[2,16,96,256]{3,2,0,1:T(8,128)(2,1)} copy(bf16[2,16,96,256]{3,2,1,0:T(8,128)(2,1)} %bitcast.161) | data formatting | bytes 3145728 | tf_op jit(solution)/shard_map/reshape | solution.py:83
  133.4 4.9 %all-to-all-start.2 = ((bf16[2,16,96,256]{3,2,0,1:T(8,128)(2,1)}), bf16[2,16,96,256]{3,2,0,1:T(8,128)(2,1)}, u32[]{:S(2)}, u32[]{:S(2)}) async-start(bf16[2,16,96,256]{3,2,0,1:T(8,128)(2,1)} %copy.153), calls=%async_computation.2 | async-start | bytes 3145728 | tf_op jit(solution)/shard_map/all_to_all | solution.py:84
  140.3 5.1 %fusion.25 = bf16[2,1536,256]{1,2,0:T(8,128)(2,1)} fusion(bf16[4,256,1536]{2,1,0:T(8,128)(2,1)} %param.13, pred[4,256]{1,0:T(4,128)(4,1)S(1)} %iota_compare_fusion.2, f32[2]{0:T(128)S(1)} %and_select_fusion.1, bf16[4,256,256]{1,2,0:T(8,128)(2,1)} %copy.155, bf16[2,4]{1,0:T(2,128)(2,1)S(1)} %compare_convert_fusion), kind=kOutput, calls=%fused_computation.36 | convolution fusion | flops 1614282752 | bytes 5243928 | tf_op jit(solution)/shard_map/ufd,sufr->sdr/dot_general | solution.py:20
  148.0 2.7 %copy.157 = bf16[2,16,96,256]{3,2,0,1:T(8,128)(2,1)} copy(bf16[2,16,96,256]{3,2,1,0:T(8,128)(2,1)} %bitcast.162) | data formatting | bytes 3145728 | tf_op jit(solution)/shard_map/reshape | solution.py:83
  150.7 23.9 %all-to-all-done.2 = bf16[2,16,96,256]{3,2,0,1:T(8,128)(2,1)} async-done(((bf16[2,16,96,256]{3,2,0,1:T(8,128)(2,1)}), bf16[2,16,96,256]{3,2,0,1:T(8,128)(2,1)}, u32[]{:S(2)}, u32[]{:S(2)}) %all-to-all-start.2) | async-done | bytes 1572896 | tf_op jit(solution)/shard_map/all_to_all | solution.py:84
  174.6 4.9 %all-to-all-start.3 = ((bf16[2,16,96,256]{3,2,0,1:T(8,128)(2,1)}), bf16[2,16,96,256]{3,2,0,1:T(8,128)(2,1)}, u32[]{:S(2)}, u32[]{:S(2)}) async-start(bf16[2,16,96,256]{3,2,0,1:T(8,128)(2,1)} %copy.157), calls=%async_computation.3 | async-start | bytes 3145728 | tf_op jit(solution)/shard_map/all_to_all | solution.py:84
  179.5 4.6 %multiply_reduce_fusion = (f32[4,256]{1,0:T(4,128)S(1)}, f32[4,256]{1,0:T(4,128)S(1)}, f32[4,256,1536]{2,1,0:T(8,128)S(1)}) fusion(f32[1536]{0:T(1024)S(1)} %copy-done.5, f32[4,256]{1,0:T(4,128)S(1)} %add_rsqrt_fusion, f32[4,256]{1,0:T(4,128)S(1)} %broadcast_multiply_fusion.2, bf16[4,256,1536]{2,1,0:T(8,128)(2,1)S(1)} %copy-done.1, ...), kind=kOutput, calls=%fused_computation.22 | convolution fusion | flops 817887232 | bytes 13129732 | tf_op jit(solution)/shard_map/ufr,udr->ufd/dot_general | solution.py:29
  184.1 3.9 %fusion.10 = bf16[4,256,1536]{2,1,0:T(8,128)(2,1)} fusion(bf16[4,256,1536]{2,1,0:T(8,128)(2,1)S(1)} %copy-done.1, bf16[4,256,1536]{2,1,0:T(8,128)(2,1)S(1)} %copy-done.4, f32[4,256,1536]{2,1,0:T(8,128)S(1)} %get-tuple-element.29, f32[4,256]{1,0:T(4,128)S(1)} %broadcast_multiply_fusion, f32[4,256]{1,0:T(4,128)S(1)} %broadcast_multiply_fusion.1, ...), kind=kLoop, calls=%fused_computation.20 | loop fusion | flops 17301504 | bytes 15751168 | tf_op jit(solution)/shard_map/convert_element_type | solution.py:36
  192.6 7.8 %copy.159 = bf16[160,96,256]{2,1,0:T(8,128)(2,1)} copy(bf16[160,96,256]{2,0,1:T(8,128)(2,1)S(1)} %convolution_convert_fusion.1) | data formatting | bytes 15728640
  200.4 15.4 %all-to-all-done.3 = bf16[2,16,96,256]{3,2,0,1:T(8,128)(2,1)} async-done(((bf16[2,16,96,256]{3,2,0,1:T(8,128)(2,1)}), bf16[2,16,96,256]{3,2,0,1:T(8,128)(2,1)}, u32[]{:S(2)}, u32[]{:S(2)}) %all-to-all-start.3) | async-done | bytes 1572896 | tf_op jit(solution)/shard_map/all_to_all | solution.py:84
  220.4 8.1 %copy.160 = bf16[160,96,256]{2,1,0:T(8,128)(2,1)} copy(bf16[160,96,256]{2,0,1:T(8,128)(2,1)S(1)} %convolution_convert_fusion) | data formatting | bytes 15728640
  (66 shorter events, 36.8 us)
Async XLA Ops:
  10.7 16.9 %copy-start = (s32[16,2]{0,1:T(2,128)S(1)}, s32[16,2]{0,1:T(2,128)}, u32[]{:S(2)}) copy-start(s32[16,2]{0,1:T(2,128)} %param.17) | copy-start | bytes 388
  21.0 42.8 %all-to-all-start = ((bf16[16,2,1,96,256]{4,3,1,2,0:T(8,128)(2,1)}), bf16[16,2,1,96,256]{4,3,1,2,0:T(8,128)(2,1)}, u32[]{:S(2)}, u32[]{:S(2)}) async-start(bf16[16,2,1,96,256]{4,3,1,2,0:T(8,128)(2,1)} %fusion.53), calls=%async_computation | async-start | bytes 3145728 | tf_op jit(solution)/shard_map/all_to_all | solution.py:65
  27.8 41.0 %copy-start.6 = (s32[64]{0:T(128)S(1)}, s32[64]{0:T(128)}, u32[]{:S(2)}) copy-start(s32[64]{0:T(128)} %param.18) | copy-start | bytes 772
  27.8 41.9 %copy-start.7 = (s32[64]{0:T(128)S(1)}, s32[64]{0:T(128)}, u32[]{:S(2)}) copy-start(s32[64]{0:T(128)} %param.19) | copy-start | bytes 772
  27.8 42.9 %copy-start.1 = (bf16[4,256,1536]{2,1,0:T(8,128)(2,1)S(1)}, bf16[4,256,1536]{2,1,0:T(8,128)(2,1)}, u32[]{:S(2)}) copy-start(bf16[4,256,1536]{2,1,0:T(8,128)(2,1)} %param.12) | copy-start | bytes 9437188
  63.9 41.2 %all-to-all-start.1 = ((bf16[2,16,96,256]{3,2,0,1:T(8,128)(2,1)}), bf16[2,16,96,256]{3,2,0,1:T(8,128)(2,1)}, u32[]{:S(2)}, u32[]{:S(2)}) async-start(bf16[2,16,96,256]{3,2,0,1:T(8,128)(2,1)} %copy.149), calls=%async_computation.1 | async-start | bytes 3145728 | tf_op jit(solution)/shard_map/all_to_all | solution.py:63
  111.6 3.8 %copy-start.5 = (f32[1536]{0:T(1024)S(1)}, f32[1536]{0:T(1024)}, u32[]{:S(2)}) copy-start(f32[1536]{0:T(1024)} %param.14) | copy-start | bytes 18436
  115.4 4.4 %copy-start.2 = (bf16[4,1536,256]{2,1,0:T(8,128)(2,1)S(1)}, bf16[4,1536,256]{2,1,0:T(8,128)(2,1)}, u32[]{:S(2)}) copy-start(bf16[4,1536,256]{2,1,0:T(8,128)(2,1)} %gather_fusion.3) | copy-start | bytes 9437188
  115.4 4.4 %copy-start.3 = (bf16[4,256,1536]{2,1,0:T(8,128)(2,1)S(1)}, bf16[4,256,1536]{2,1,0:T(8,128)(2,1)}, u32[]{:S(2)}) copy-start(bf16[4,256,1536]{2,1,0:T(8,128)(2,1)} %param.13) | copy-start | bytes 9437188
  133.4 41.2 %all-to-all-start.2 = ((bf16[2,16,96,256]{3,2,0,1:T(8,128)(2,1)}), bf16[2,16,96,256]{3,2,0,1:T(8,128)(2,1)}, u32[]{:S(2)}, u32[]{:S(2)}) async-start(bf16[2,16,96,256]{3,2,0,1:T(8,128)(2,1)} %copy.153), calls=%async_computation.2 | async-start | bytes 3145728 | tf_op jit(solution)/shard_map/all_to_all | solution.py:84
  174.6 41.2 %all-to-all-start.3 = ((bf16[2,16,96,256]{3,2,0,1:T(8,128)(2,1)}), bf16[2,16,96,256]{3,2,0,1:T(8,128)(2,1)}, u32[]{:S(2)}, u32[]{:S(2)}) async-start(bf16[2,16,96,256]{3,2,0,1:T(8,128)(2,1)} %copy.157), calls=%async_computation.3 | async-start | bytes 3145728 | tf_op jit(solution)/shard_map/all_to_all | solution.py:84
  179.5 4.6 %copy-start.4 = (bf16[4,256,1536]{2,1,0:T(8,128)(2,1)S(1)}, bf16[4,256,1536]{2,1,0:T(8,128)(2,1)}, u32[]{:S(2)}) copy-start(bf16[4,256,1536]{2,1,0:T(8,128)(2,1)} %param.13) | copy-start | bytes 9437188
